TPU v7x, 256 devices: a whole 4x4x8 slice. The times are simulated.
256 devices in a mesh: section: 2 (over core), tok: 32 (over z, y), rep: 4 (over x).
Axes of the slice: x: 4, y: 4, z: 8, core: 2. Of those that a mesh axis runs over, the one named last changes fastest.
Arguments:
- inputs: bfloat16 [2, 4096, 1024], P(None, 'tok')
- segment_ids: int32 [2, 4096], replicated, may hold values from 0 to 7, as said below
- picks: int32 [2, 4096, 2], P(None, 'tok'), may hold values from 0 to 15, all different within a row; in each aligned block of 128 rows (0 to 127, 128 to 255, ..., all dimensions but the last counted through in order) at most 20 rows name the same one
- page_table: int32 [2, 32], replicated, may hold values from 0 to 31, each once within a row
- norm_gains: float32 [2, 2, 1024], P('section'), may hold values from 0.1 to 1.9
- attn_qkv: bfloat16 [2, 1024, 3, 1024], P('section', None, None, 'rep')
- attn_out: bfloat16 [2, 1024, 1024], P('section', 'rep'), may hold values from -0.1875 to 0.1875
- router: bfloat16 [2, 1024, 16], P('section')
- expert_in: bfloat16 [2, 32, 1024, 2, 1408], P('section', 'tok', None, None, 'rep'), may hold values from -0.1875 to 0.1875
- expert_out: bfloat16 [2, 32, 1408, 1024], P('section', 'tok', 'rep')
Outputs:
- layer_out: bfloat16 [2, 2, 4096, 1024], P('section', None, 'tok')
- kv_pages: bfloat16 [2, 2, 32, 128, 2, 1024], P('section', None, 'tok', None, None, 'rep')
Inputs may be any that keep to these rules, and one draw needn't show every extreme that they name: `picks`: within the tokens of one index of tok in one micro-batch, at most 20 tokens pick one expert, and some expert is picked by exactly 20. `segment_ids`: ids never fall along a micro-batch; every prompt has at least one token, a prompt spans at most 2048 tokens and one spans exactly 2048. `page_table`: each row is a permutation.
All inputs are finite; a program needn't handle non-finite values.
Results may differ from a plain program's by a relative error of at most 0.034.
Values may be sent and summed in bfloat16 or wider, within the bound.
No kernel may reach another device: no remote copies, remote signals or barrier semaphores. Data moves between devices by JAX's collectives and lax.ppermute only.
A program may use at most 128 MiB of HBM per device.

v0:
```python
import jax
import jax.numpy as jnp
from jax import lax
from jax.sharding import PartitionSpec as P

HEAD_DIM = 64
TOP = 2
PAGE = 128
CAP = 20
NEG_FILL = -1e30


def shifted(value, axis, steps):
    count = lax.axis_size(axis)
    first, last = (max(0, -steps), min(count, count - steps))
    return lax.ppermute(value, axis, [(source, source + steps) for source in range(first, last)])


def rms_scale(values, gains):
    return values * lax.rsqrt(jnp.mean(values * values, axis=-1, keepdims=True) + 1e-06) * gains


def attend(carry, queries, keys_vals, seg_query, pos_query, seg_key, pos_key):
    run_max, run_sum, run_acc = carry
    heads_here = run_acc.shape[0]
    head_size = run_acc.shape[2]
    rows_key = keys_vals.shape[0]
    key_part = keys_vals[:, 0].reshape(rows_key, heads_here, head_size)
    val_part = keys_vals[:, 1].reshape(rows_key, heads_here, head_size).astype(jnp.float32)
    scores = jnp.einsum(
        "thd,nhd->htn", queries, key_part, preferred_element_type=jnp.float32
    ) * head_size ** (-0.5)
    visible = (seg_query[:, None] == seg_key[None, :]) & (pos_query[:, None] >= pos_key[None, :])
    masked = jnp.where(visible[None], scores, NEG_FILL)
    new_max = jnp.maximum(run_max, jnp.max(masked, axis=-1))
    weights = jnp.where(visible[None], jnp.exp(masked - new_max[..., None]), 0.0)
    decay = jnp.exp(run_max - new_max)
    run_sum = run_sum * decay + jnp.sum(weights, axis=-1)
    run_acc = run_acc * decay[..., None] + jnp.einsum(
        "htn,nhd->htd", weights, val_part, precision=lax.Precision.HIGHEST
    )
    return (new_max, run_sum, run_acc)


def place_pages(pages, keys_vals, table_row, tok_index):
    rows_here = keys_vals.shape[0]
    blocks_dev = pages.shape[0]
    page_rows = pages.shape[1]
    block_ids = jnp.arange(table_row.shape[0], dtype=jnp.int32)
    wanted = tok_index * blocks_dev + 0
    source = jnp.sum(jnp.where(table_row == wanted, block_ids, 0))
    offset = source * page_rows
    inside = (offset >= 0) & (offset + page_rows <= rows_here)
    block = lax.dynamic_slice_in_dim(
        keys_vals, jnp.clip(offset, 0, rows_here - page_rows), page_rows, 0
    )
    updated = [jnp.where(inside, block, pages[0])]
    return jnp.stack(updated)


def one_layer(layer_in, seg_all, table_row, pick_rows, gains, w_qkv, w_out, w_router, w_in, w_down):
    tok_index = lax.axis_index("tok")
    tok_count = lax.axis_size("tok")
    tok_rows = layer_in.shape[0]
    width = layer_in.shape[1]
    col_width = w_qkv.shape[1] // 3
    head_count = col_width // HEAD_DIM
    experts_all = w_router.shape[1]
    local_pieces = w_in.shape[0]
    split_count = local_pieces * tok_count // experts_all
    blocks_dev = tok_rows // PAGE
    row_ids = jnp.arange(tok_rows, dtype=jnp.int32)
    pos_query = tok_index * tok_rows + row_ids
    seg_query = lax.dynamic_slice_in_dim(seg_all, tok_index * tok_rows, tok_rows)
    resid = layer_in.astype(jnp.float32)
    normed = rms_scale(resid, gains[0]).astype(jnp.bfloat16)
    projected = jnp.dot(normed, w_qkv, preferred_element_type=jnp.float32).astype(jnp.bfloat16)
    projected = projected.reshape(tok_rows, 3, col_width)
    queries = projected[:, 0].reshape(tok_rows, head_count, HEAD_DIM)
    keys_vals = projected[:, 1:]
    soft_init = (
        jnp.full((head_count, tok_rows), NEG_FILL, jnp.float32),
        jnp.zeros((head_count, tok_rows), jnp.float32),
        jnp.zeros((head_count, tok_rows, HEAD_DIM), jnp.float32),
    )
    empty_pages = jnp.zeros((blocks_dev, PAGE, 2, col_width), jnp.bfloat16)
    piece = lax.all_gather(keys_vals, "tok", axis=0, tiled=True)
    rows_key = piece.shape[0]
    step_rows = 1024
    while rows_key % step_rows != 0:
        step_rows = step_rows // 2
    turns = rows_key // step_rows

    def key_block(index, soft_now):
        start = index * step_rows
        block = lax.dynamic_slice_in_dim(piece, start, step_rows, 0)
        seg_key = lax.dynamic_slice_in_dim(seg_all, start, step_rows)
        pos_key = start + jnp.arange(step_rows, dtype=jnp.int32)
        return attend(soft_now, queries, block, seg_query, pos_query, seg_key, pos_key)

    soft_next = lax.fori_loop(0, turns, key_block, soft_init)
    pages = place_pages(empty_pages, piece, table_row, tok_index)
    run_max, run_sum, run_acc = soft_next
    context = (
        (run_acc / run_sum[..., None])
        .transpose(1, 0, 2)
        .reshape(tok_rows, col_width)
        .astype(jnp.bfloat16)
    )
    attn_part = jnp.dot(context, w_out, preferred_element_type=jnp.float32)
    mid = resid + lax.psum(attn_part, "rep")
    normed_mid = rms_scale(mid, gains[1]).astype(jnp.bfloat16)
    logits = jnp.dot(normed_mid, w_router, preferred_element_type=jnp.float32)
    expert_ids = jnp.arange(experts_all, dtype=jnp.int32)
    chosen = (pick_rows[:, :, None] == expert_ids[None, None, :]).astype(jnp.int32)
    picked_logit = jnp.sum(chosen.astype(jnp.float32) * logits[:, None, :], axis=-1)
    top_logit = jnp.max(picked_logit, axis=-1, keepdims=True)
    raised = jnp.exp(picked_logit - top_logit)
    gate_vals = raised / jnp.sum(raised, axis=-1, keepdims=True)
    ordered = chosen.transpose(1, 0, 2).reshape(TOP * tok_rows, experts_all)
    slot_of = jnp.sum((jnp.cumsum(ordered, axis=0) - 1) * ordered, axis=-1)
    flat_slot = pick_rows.T.reshape(TOP * tok_rows) * CAP + slot_of
    slot_ids = jnp.arange(experts_all * CAP, dtype=jnp.int32)
    hits = (flat_slot[:, None] == slot_ids[None, :]).astype(jnp.int32)
    hits = jnp.sum(hits.reshape(TOP, tok_rows, experts_all * CAP), axis=0).astype(jnp.bfloat16)
    dispatch = lax.dot_general(
        hits, normed_mid, (((0,), (0,)), ((), ())), preferred_element_type=jnp.float32
    ).astype(jnp.bfloat16)
    copies = jnp.broadcast_to(
        dispatch.reshape(experts_all, 1, CAP, width), (experts_all, split_count, CAP, width)
    )
    copies = copies.reshape(tok_count, local_pieces, CAP, width)
    act = jnp.einsum(
        "secd,edgf->secgf",
        lax.all_to_all(copies, "tok", split_axis=0, concat_axis=0, tiled=True),
        w_in,
        preferred_element_type=jnp.float32,
    )
    hidden = (jax.nn.gelu(act[..., 0, :]) * act[..., 1, :]).astype(jnp.bfloat16)
    returned = lax.all_to_all(
        jnp.einsum("secf,efd->secd", hidden, w_down, preferred_element_type=jnp.float32).astype(
            jnp.bfloat16
        ),
        "tok",
        split_axis=0,
        concat_axis=0,
        tiled=True,
    )
    summed = jnp.sum(
        returned.reshape(experts_all, split_count, CAP, width).astype(jnp.float32), axis=1
    )
    summed = summed.reshape(experts_all * CAP, width)
    gathered = jnp.take(summed, flat_slot, axis=0).reshape(TOP, tok_rows, width)
    expert_local = jnp.sum(gate_vals.T[:, :, None] * gathered, axis=0)
    expert_total = lax.psum(expert_local, "rep")
    layer_result = (mid + expert_total).astype(jnp.bfloat16)
    return (layer_result, pages)


def per_device(
    inputs,
    segment_ids,
    picks,
    page_table,
    norm_gains,
    attn_qkv,
    attn_out,
    router,
    expert_in,
    expert_out,
):
    section_index = lax.axis_index("section")
    is_first = section_index == 0
    width = inputs.shape[2]
    own = (
        norm_gains[0],
        attn_qkv[0].reshape(width, -1),
        attn_out[0],
        router[0],
        expert_in[0],
        expert_out[0],
    )
    swap = [(0, 1), (1, 0)]
    other = tuple((lax.ppermute(w, "section", swap) for w in own))
    weights_of = [
        tuple((jnp.where(is_first, a, b) for a, b in zip(own, other))),
        tuple((jnp.where(is_first, b, a) for a, b in zip(own, other))),
    ]
    micro = section_index
    hidden = lax.dynamic_index_in_dim(inputs, micro, 0, keepdims=False)
    seg_all = lax.dynamic_index_in_dim(segment_ids, micro, 0, keepdims=False)
    table_row = lax.dynamic_index_in_dim(page_table, micro, 0, keepdims=False)
    pick_rows = lax.dynamic_index_in_dim(picks, micro, 0, keepdims=False)
    results = []
    for layer in range(2):
        hidden, pages = one_layer(hidden, seg_all, table_row, pick_rows, *weights_of[layer])
        results.append((hidden, pages))
    (res0, pages0), (res1, pages1) = results
    got0 = lax.ppermute(res0, "section", [(1, 0)])
    gotp0 = lax.ppermute(pages0, "section", [(1, 0)])
    got1 = lax.ppermute(res1, "section", [(0, 1)])
    gotp1 = lax.ppermute(pages1, "section", [(0, 1)])
    outputs = jnp.where(is_first, jnp.stack([res0, got0]), jnp.stack([got1, res1]))
    page_out = jnp.where(is_first, jnp.stack([pages0, gotp0]), jnp.stack([gotp1, pages1]))
    return (outputs[None], page_out[None])


def solution(mesh):
    return jax.shard_map(
        per_device,
        mesh=mesh,
        in_specs=(
            P(None, "tok", None),
            P(),
            P(None, "tok", None),
            P(),
            P("section", None, None),
            P("section", None, None, "rep"),
            P("section", "rep", None),
            P("section", None, None),
            P("section", "tok", None, None, "rep"),
            P("section", "tok", "rep", None),
        ),
        out_specs=(P("section", None, "tok", None), P("section", None, "tok", None, None, "rep")),
        check_vma=False,
    )
```

profile of v0, /device:TPU:1, one launch (start us, length us, event | category | flops | bytes accessed | tf_op | source)
XLA Modules:
  0.0 634.5 jit_solution(9774270104577038417)
XLA Ops:
  7.2 1.8 copy.55
  9.0 3.3 collective-permute-start.1
  12.6 2.9 collective-permute-done
  15.5 2.1 fusion.48
  19.5 79.9 %all-gather.3.cloned.1.call-done = bf16[4096,2,256]{0,2,1:T(8,128)(2,1)} async-done(((bf16[128,2,256]{0,2,1:T(8,128)(2,1)}), bf16[4096,2,256]{0,2,1:T(8,128)(2,1)}) %all-gather.3.cloned.1.call-update) | async-done | bytes 4194320 | tf_op jit(solution)/shard_map/all_gather | solution.py:87
  99.4 17.1 %while.36 = (s32[]{:T(128)}, f32[4,128]{1,0:T(4,128)S(1)}, f32[4,128]{1,0:T(4,128)S(1)}, f32[4,128,64]{1,2,0:T(8,128)S(1)}, s32[128]{0:T(128)S(1)}, /*index=5*/s...) while((s32[]{:T(128)}, f32[4,128]{1,0:T(4,128)S(1)}, ...), condition=%wide.region_4.5_spmd.clone, body=%wide.region_1.4_spmd.clone.sunk | while | flops 476548736 | bytes 10344167 | solution.py:101
  99.7 1.3 constant_dynamic-slice_fusion.9
  102.2 1.4 fusion.180
  104.0 1.3 constant_dynamic-slice_fusion.9
  106.5 1.4 fusion.180
  108.3 1.3 constant_dynamic-slice_fusion.9
  110.8 1.4 fusion.180
  112.6 1.3 constant_dynamic-slice_fusion.9
  115.1 1.4 fusion.180
  116.6 1.1 fusion.86
  118.0 49.1 %all-reduce.5.cloned.1.call-done = f32[128,1024]{1,0:T(8,128)} async-done(((f32[128,1024]{1,0:T(8,128)}), f32[128,1024]{1,0:T(8,128)}) %all-reduce.5.cloned.1.call-update) | async-done | bytes 524304 | tf_op jit(solution)/shard_map/psum | solution.py:111
  167.2 1.2 multiply_reduce_fusion.3
  168.4 1.2 multiply_convert_fusion.1
  170.0 1.4 broadcast_in_dim.165
  171.5 9.7 %all-to-all-start = ((bf16[32,1,20,1024]{3,2,1,0:T(8,128)(2,1)}), bf16[32,1,20,1024]{3,2,1,0:T(8,128)(2,1)S(1)}, u32[]{:S(2)}, u32[]{:S(2)}) async-start(bf16[32,1,20,1024]{3,2,1,0:T(8,128)(2,1)} %bitcast.29), calls=%async_computation | async-start | bytes 3145728 | tf_op jit(solution)/shard_map/all_to_all | solution.py:135
  181.2 3.2 collective-permute-start.5
  184.7 2.9 collective-permute-done.5
  187.6 28.6 %all-to-all-done = bf16[32,1,20,1024]{3,2,1,0:T(8,128)(2,1)S(1)} async-done(((bf16[32,1,20,1024]{3,2,1,0:T(8,128)(2,1)}), bf16[32,1,20,1024]{3,2,1,0:T(8,128)(2,1)S(1)}, u32[]{:S(2)}, u32[]{:S(2)}) %all-to-all-start) | async-done | bytes 1310752 | tf_op jit(solution)/shard_map/all_to_all | solution.py:135
  216.2 3.6 convolution_bitcast_fusion.1
  219.8 2.3 fusion.42
  222.1 2.0 copy.59
  224.1 7.5 %all-to-all-start.1 = ((bf16[32,1,20,1024]{3,2,1,0:T(8,128)(2,1)}), bf16[32,1,20,1024]{3,2,1,0:T(8,128)(2,1)S(1)}, u32[]{:S(2)}, u32[]{:S(2)}) async-start(bf16[32,1,20,1024]{3,2,1,0:T(8,128)(2,1)} %copy.59), calls=%async_computation.1 | async-start | bytes 3145728 | tf_op jit(solution)/shard_map/all_to_all | solution.py:140
  231.7 2.9 collective-permute-start.3
  235.6 31.5 %all-to-all-done.1 = bf16[32,1,20,1024]{3,2,1,0:T(8,128)(2,1)S(1)} async-done(((bf16[32,1,20,1024]{3,2,1,0:T(8,128)(2,1)}), bf16[32,1,20,1024]{3,2,1,0:T(8,128)(2,1)S(1)}, u32[]{:S(2)}, u32[]{:S(2)}) %all-to-all-start.1) | async-done | bytes 1310752 | tf_op jit(solution)/shard_map/all_to_all | solution.py:140
  267.7 1.1 gather_fusion
  268.9 0.9 multiply_reduce_fusion.1
  269.9 47.1 %all-reduce.7.cloned.1.call-done = f32[128,1024]{1,0:T(8,128)} async-done(((f32[128,1024]{1,0:T(8,128)}), f32[128,1024]{1,0:T(8,128)}) %all-reduce.7.cloned.1.call-update) | async-done | bytes 524304 | tf_op jit(solution)/shard_map/psum | solution.py:155
  317.0 1.2 fusion.78
  319.9 84.1 %all-gather.5.cloned.1.call-done = bf16[4096,2,256]{0,2,1:T(8,128)(2,1)} async-done(((bf16[128,2,256]{0,2,1:T(8,128)(2,1)}), bf16[4096,2,256]{0,2,1:T(8,128)(2,1)}) %all-gather.5.cloned.1.call-update) | async-done | bytes 4194320 | tf_op jit(solution)/shard_map/all_gather | solution.py:87
  404.0 17.1 %while.37 = (s32[]{:T(128)}, f32[4,128]{1,0:T(4,128)S(1)}, f32[4,128]{1,0:T(4,128)S(1)}, f32[4,128,64]{1,2,0:T(8,128)S(1)}, s32[128]{0:T(128)S(1)}, /*index=5*/s...) while((s32[]{:T(128)}, f32[4,128]{1,0:T(4,128)S(1)}, ...), condition=%wide.region_21.23_spmd.clone, body=%wide.region_18.22_spmd.clone.sunk | while | flops 476548736 | bytes 10344167 | solution.py:101
  404.4 1.3 constant_dynamic-slice_fusion.10
  406.9 1.4 fusion.187
  408.7 1.3 constant_dynamic-slice_fusion.10
  411.2 1.4 fusion.187
  413.0 1.3 constant_dynamic-slice_fusion.10
  415.4 1.4 fusion.187
  417.3 1.3 constant_dynamic-slice_fusion.10
  419.7 1.4 fusion.187
  421.2 1.1 fusion.84
  422.3 49.5 %all-reduce.9.cloned.1.call-done = f32[128,1024]{1,0:T(8,128)} async-done(((f32[128,1024]{1,0:T(8,128)}), f32[128,1024]{1,0:T(8,128)}) %all-reduce.9.cloned.1.call-update) | async-done | bytes 524304 | tf_op jit(solution)/shard_map/psum | solution.py:111
  471.8 1.2 multiply_reduce_fusion.2
  473.0 1.2 multiply_convert_fusion
  474.8 45.7 %all_to_all.20 = bf16[32,1,20,1024]{3,2,1,0:T(8,128)(2,1)S(1)} all-to-all(bf16[32,1,20,1024]{3,2,1,0:T(8,128)(2,1)S(1)} %bitcast.258), channel_id=1, replica_groups=mesh['section'=2,'tok'=32,'rep'=4] {'tok'}, dimensions={0} | all-to-all | bytes 2621440 | tf_op jit(solution)/shard_map/all_to_all | solution.py:135
  520.5 1.8 convolution_bitcast_fusion
  522.3 1.0 fusion.43
  523.4 2.0 copy.64
  525.3 6.1 all-to-all-start.3
  531.7 31.8 %all-to-all-done.3 = bf16[32,1,20,1024]{3,2,1,0:T(8,128)(2,1)S(1)} async-done(((bf16[32,1,20,1024]{3,2,1,0:T(8,128)(2,1)}), bf16[32,1,20,1024]{3,2,1,0:T(8,128)(2,1)S(1)}, u32[]{:S(2)}, u32[]{:S(2)}) %all-to-all-start.3) | async-done | bytes 1310752 | tf_op jit(solution)/shard_map/all_to_all | solution.py:140
  564.0 1.1 gather_fusion.1
  565.3 0.9 multiply_reduce_fusion
  567.5 1.1 fusion.109
  568.6 9.9 %collective-permute-start.8 = (bf16[1,128,2,256]{1,3,2,0:T(8,128)(2,1)S(1)}, bf16[1,128,2,256]{1,3,2,0:T(8,128)(2,1)S(1)}, u32[]{:S(2)}, u32[]{:S(2)}) collective-permute-start(bf16[1,128,2,256]{1,3,2,0:T(8,128)(2,1)S(1)} %get-tuple-element.462), channel_id=1, source_target_pairs={{128,0},{129,1},{130,2},{131,3},{132,4},{133,5},{134,6},{135,7},{1... | collective-permute-start | bytes 393224 | tf_op jit(solution)/shard_map/ppermute | solution.py:200
  578.5 1.3 collective-permute-start.6
  579.8 37.5 %all-reduce.11.cloned.1.call-done = f32[128,1024]{1,0:T(8,128)} async-done(((f32[128,1024]{1,0:T(8,128)}), f32[128,1024]{1,0:T(8,128)}) %all-reduce.11.cloned.1.call-update) | async-done | bytes 524304 | tf_op jit(solution)/shard_map/psum | solution.py:155
  617.3 1.1 add_convert_fusion
  618.4 1.3 collective-permute-start.7
  619.7 1.1 fusion.111
  620.8 1.3 collective-permute-start.9
  622.1 3.7 collective-permute-done.9
  (192 shorter events, 22.9 us)
Async XLA Ops:
  7.2 12.2 %copy-start = (s32[2,4096]{1,0:T(2,128)S(1)}, s32[2,4096]{1,0:T(2,128)}, u32[]{:S(2)}) copy-start(s32[2,4096]{1,0:T(2,128)} %param.17) | copy-start | bytes 98308
  7.2 5.1 copy-start.13
  7.2 5.2 copy-start.4
  7.2 92.2 %all-gather.3.cloned.1.call-start = ((), (), s32[]{:S(2)}) async-start(), calls=%async_computation.4 | async-start | bytes 4325376 | tf_op jit(solution)/shard_map/all_gather | solution.py:87
  9.0 8.7 %copy-start.10 = (bf16[1,1024,3,256]{1,3,2,0:T(8,128)(2,1)}, bf16[1,1024,3,256]{1,3,2,0:T(8,128)(2,1)S(1)}, u32[]{:S(2)}) copy-start(bf16[1,1024,3,256]{1,3,2,0:T(8,128)(2,1)S(1)} %copy.55) | copy-start | bytes 4718596
  9.0 6.5 %collective-permute-start.1 = (bf16[1024,768]{0,1:T(8,128)(2,1)S(1)}, bf16[1024,768]{0,1:T(8,128)(2,1)}, u32[]{:S(2)}, u32[]{:S(2)}) collective-permute-start(bf16[1024,768]{0,1:T(8,128)(2,1)S(1)} %bitcast.264), channel_id=1, source_target_pairs={{0,128},{128,0},{1,129},{129,1},{2,130},{130,2},{3,131},{131,3},{4... | collective-permute-start | bytes 4718600 | tf_op jit(solution)/shard_map/ppermute | solution.py:184
  12.3 3.2 collective-permute-start
  15.5 3.1 copy-start.6
  15.5 3.2 copy-start.14
  18.6 148.6 %all-reduce.5.cloned.1.call-start = ((), (), s32[]{:S(2)}) async-start(), calls=%async_computation.5 | async-start | bytes 1048576 | tf_op jit(solution)/shard_map/psum | solution.py:111
  18.6 97.9 %collective-permute-start.2 = (bf16[256,1024]{1,0:T(8,128)(2,1)S(1)}, bf16[256,1024]{1,0:T(8,128)(2,1)S(1)}, u32[]{:S(2)}, u32[]{:S(2)}) collective-permute-start(bf16[256,1024]{1,0:T(8,128)(2,1)S(1)} %bitcast.263), channel_id=1, source_target_pairs={{0,128},{128,0},{1,129},{129,1},{2,130},{130,2},{3,131},{131,3},{4... | collective-permute-start | bytes 1572872 | tf_op jit(solution)/shard_map/ppermute | solution.py:184
  116.6 51.8 %copy-start.8 = (bf16[256,1024]{1,0:T(8,128)(2,1)}, bf16[256,1024]{1,0:T(8,128)(2,1)S(1)}, u32[]{:S(2)}) copy-start(bf16[256,1024]{1,0:T(8,128)(2,1)S(1)} %collective-permute-done.2) | copy-start | bytes 1572868
  171.5 13.0 %copy-start.17 = (bf16[1,1,352,1024]{3,2,1,0:T(8,128)(2,1)S(1)}, bf16[1,1,352,1024]{3,2,1,0:T(8,128)(2,1)}, u32[]{:S(2)}) copy-start(bf16[1,1,352,1024]{3,2,1,0:T(8,128)(2,1)} %param.25) | copy-start | bytes 2162692
  171.5 44.8 %all-to-all-start = ((bf16[32,1,20,1024]{3,2,1,0:T(8,128)(2,1)}), bf16[32,1,20,1024]{3,2,1,0:T(8,128)(2,1)S(1)}, u32[]{:S(2)}, u32[]{:S(2)}) async-start(bf16[32,1,20,1024]{3,2,1,0:T(8,128)(2,1)} %bitcast.29), calls=%async_computation | async-start | bytes 3145728 | tf_op jit(solution)/shard_map/all_to_all | solution.py:135
  181.2 6.4 %collective-permute-start.5 = (bf16[1,1024,2,352]{1,3,2,0:T(8,128)(2,1)}, bf16[1,1024,2,352]{1,3,2,0:T(8,128)(2,1)}, u32[]{:S(2)}, u32[]{:S(2)}) collective-permute-start(bf16[1,1024,2,352]{1,3,2,0:T(8,128)(2,1)} %bitcast.285), channel_id=1, source_target_pairs={{0,128},{128,0},{1,129},{129,1},{2,130},{130,2},{3,131},{131,3},{4... | collective-permute-start | bytes 4325384 | tf_op jit(solution)/shard_map/ppermute | solution.py:184
  184.4 35.4 %collective-permute-start.4 = (bf16[1,352,1024]{2,1,0:T(8,128)(2,1)S(1)}, bf16[1,352,1024]{2,1,0:T(8,128)(2,1)}, u32[]{:S(2)}, u32[]{:S(2)}) collective-permute-start(bf16[1,352,1024]{2,1,0:T(8,128)(2,1)S(1)} %bitcast.286), channel_id=1, source_target_pairs={{0,128},{128,0},{1,129},{129,1},{2,130},{130,2},{3,131},{131,3},{4... | collective-permute-start | bytes 2162696 | tf_op jit(solution)/shard_map/ppermute | solution.py:184
  224.1 7.6 %copy-start.12 = (bf16[1,1024,16]{1,2,0:T(8,128)(2,1)S(1)}, bf16[1,1024,16]{1,2,0:T(8,128)(2,1)}, u32[]{:S(2)}) copy-start(bf16[1,1024,16]{1,2,0:T(8,128)(2,1)} %param.23) | copy-start | bytes 98308
  224.1 43.1 %all-to-all-start.1 = ((bf16[32,1,20,1024]{3,2,1,0:T(8,128)(2,1)}), bf16[32,1,20,1024]{3,2,1,0:T(8,128)(2,1)S(1)}, u32[]{:S(2)}, u32[]{:S(2)}) async-start(bf16[32,1,20,1024]{3,2,1,0:T(8,128)(2,1)} %copy.59), calls=%async_computation.1 | async-start | bytes 3145728 | tf_op jit(solution)/shard_map/all_to_all | solution.py:140
  231.6 85.4 %all-reduce.7.cloned.1.call-start = ((), (), s32[]{:S(2)}) async-start(), calls=%async_computation.6 | async-start | bytes 1048576 | tf_op jit(solution)/shard_map/psum | solution.py:155
  231.7 3.7 collective-permute-start.3
  268.7 48.3 %copy-start.3 = (f32[128,1024]{1,0:T(8,128)S(1)}, f32[128,1024]{1,0:T(8,128)}, u32[]{:S(2)}) copy-start(f32[128,1024]{1,0:T(8,128)} %all-reduce.5.cloned.1.call-done) | copy-start | bytes 1572868
  268.8 48.3 %copy-start.5 = (bf16[2,128,1024]{2,1,0:T(8,128)(2,1)S(1)}, bf16[2,128,1024]{2,1,0:T(8,128)(2,1)}, u32[]{:S(2)}) copy-start(bf16[2,128,1024]{2,1,0:T(8,128)(2,1)} %param.16) | copy-start | bytes 1572868
  268.9 49.3 %copy-start.11 = (bf16[1,1024,3,256]{1,3,2,0:T(8,128)(2,1)S(1)}, bf16[1,1024,3,256]{1,3,2,0:T(8,128)(2,1)}, u32[]{:S(2)}) copy-start(bf16[1,1024,3,256]{1,3,2,0:T(8,128)(2,1)} %copy-done.10) | copy-start | bytes 4718596
  269.9 134.2 %all-gather.5.cloned.1.call-start = ((), (), s32[]{:S(2)}) async-start(), calls=%async_computation.7 | async-start | bytes 4325376 | tf_op jit(solution)/shard_map/all_gather | solution.py:87
  319.8 152.0 %all-reduce.9.cloned.1.call-start = ((), (), s32[]{:S(2)}) async-start(), calls=%async_computation.8 | async-start | bytes 1048576 | tf_op jit(solution)/shard_map/psum | solution.py:111
  404.0 17.2 %copy-start.7 = (bf16[1,256,1024]{2,1,0:T(8,128)(2,1)S(1)}, bf16[1,256,1024]{2,1,0:T(8,128)(2,1)}, u32[]{:S(2)}) copy-start(bf16[1,256,1024]{2,1,0:T(8,128)(2,1)} %param.22) | copy-start | bytes 1572868
  404.0 17.2 %copy-start.9 = (bf16[256,1024]{1,0:T(8,128)(2,1)S(1)}, bf16[256,1024]{1,0:T(8,128)(2,1)}, u32[]{:S(2)}) copy-start(bf16[256,1024]{1,0:T(8,128)(2,1)} %copy-done.8) | copy-start | bytes 1572868
  474.8 45.7 %copy-start.16 = (bf16[1,1,1024,2,352]{2,4,3,1,0:T(8,128)(2,1)S(1)}, bf16[1,1,1024,2,352]{2,4,3,1,0:T(8,128)(2,1)}, u32[]{:S(2)}) copy-start(bf16[1,1,1024,2,352]{2,4,3,1,0:T(8,128)(2,1)} %param.24) | copy-start | bytes 4325380
  520.5 1.8 copy-start.18
  525.3 38.2 %all-to-all-start.3 = ((bf16[32,1,20,1024]{3,2,1,0:T(8,128)(2,1)}), bf16[32,1,20,1024]{3,2,1,0:T(8,128)(2,1)S(1)}, u32[]{:S(2)}, u32[]{:S(2)}) async-start(bf16[32,1,20,1024]{3,2,1,0:T(8,128)(2,1)} %copy.64), calls=%async_computation.3 | async-start | bytes 3145728 | tf_op jit(solution)/shard_map/all_to_all | solution.py:140
  531.4 85.8 %all-reduce.11.cloned.1.call-start = ((), (), s32[]{:S(2)}) async-start(), calls=%async_computation.9 | async-start | bytes 1048576 | tf_op jit(solution)/shard_map/psum | solution.py:155
  565.1 1.1 copy-start.15
  565.1 52.2 %copy-start.2 = (f32[128,1024]{1,0:T(8,128)S(1)}, f32[128,1024]{1,0:T(8,128)}, u32[]{:S(2)}) copy-start(f32[128,1024]{1,0:T(8,128)} %all-reduce.9.cloned.1.call-done) | copy-start | bytes 1572868
  568.6 53.5 %collective-permute-start.8 = (bf16[1,128,2,256]{1,3,2,0:T(8,128)(2,1)S(1)}, bf16[1,128,2,256]{1,3,2,0:T(8,128)(2,1)S(1)}, u32[]{:S(2)}, u32[]{:S(2)}) collective-permute-start(bf16[1,128,2,256]{1,3,2,0:T(8,128)(2,1)S(1)} %get-tuple-element.462), channel_id=1, source_target_pairs={{128,0},{129,1},{130,2},{131,3},{132,4},{133,5},{134,6},{135,7},{1... | collective-permute-start | bytes 393224 | tf_op jit(solution)/shard_map/ppermute | solution.py:200
  578.5 48.3 %collective-permute-start.6 = (bf16[128,1024]{1,0:T(8,128)(2,1)S(1)}, bf16[128,1024]{1,0:T(8,128)(2,1)S(1)}, u32[]{:S(2)}, u32[]{:S(2)}) collective-permute-start(bf16[128,1024]{1,0:T(8,128)(2,1)S(1)} %get-tuple-element.448), channel_id=1, source_target_pairs={{128,0},{129,1},{130,2},{131,3},{132,4},{133,5},{134,6},{135,7},{1... | collective-permute-start | bytes 786440 | tf_op jit(solution)/shard_map/ppermute | solution.py:199
  617.3 10.4 %copy-start.1 = (s32[2,4096]{1,0:T(2,128)S(1)}, s32[2,4096]{1,0:T(2,128)}, u32[]{:S(2)}) copy-start(s32[2,4096]{1,0:T(2,128)} %param.17) | copy-start | bytes 98308
  618.4 8.3 %collective-permute-start.7 = (bf16[128,1024]{1,0:T(8,128)(2,1)S(1)}, bf16[128,1024]{1,0:T(8,128)(2,1)S(1)}, u32[]{:S(2)}, u32[]{:S(2)}) collective-permute-start(bf16[128,1024]{1,0:T(8,128)(2,1)S(1)} %add_convert_fusion), channel_id=1, source_target_pairs={{0,128},{1,129},{2,130},{3,131},{4,132},{5,133},{6,134},{7,135},{8... | collective-permute-start | bytes 786440 | tf_op jit(solution)/shard_map/ppermute | solution.py:201
  620.8 5.0 collective-permute-start.9
Sparse Core Ops, SparseCore 0:
  18.7 80.6 all-gather.2
  117.8 49.3 all-reduce.4
  270.0 46.9 all-reduce.6
  319.9 84.0 all-gather.4
  422.4 49.3 all-reduce.8
  566.3 50.8 all-reduce.10
where the time goes:
time: 636 us; the launch traced here: 634 us
  waiting for transfers between devices  450 us (71%)
  starting transfers between devices  47.2 us (7%)
  blocking collectives  45.7 us (7%)
  matrix products  30.8 us (5%)
  local copies, waits for them, and re-layouts  23.3 us (4%)
  other arithmetic  22 us (3%)
  between operations  15.4 us (2%)
    all_gather x2, waiting for transfers between devices, one_layer(): piece = lax.all_gather(keys_vals, 'tok', axis=0, tiled=True)  164 us
    psum x2, waiting for transfers between devices, one_layer(): mid = resid + lax.psum(attn_part, 'rep')  98.6 us
    psum x2, waiting for transfers between devices, one_layer(): expert_total = lax.psum(expert_local, 'rep')  84.6 us
    all_to_all x2, waiting for transfers between devices, one_layer(): lax.all_to_all(jnp.einsum('secf,efd->secd', hidden, w_down, preferred_ele...  63.3 us
    all_to_all x1, blocking collectives, one_layer(): lax.all_to_all(copies, 'tok', split_axis=0, concat_axis=0, tiled=True)  45.7 us
    all_to_all x1, waiting for transfers between devices, one_layer(): lax.all_to_all(copies, 'tok', split_axis=0, concat_axis=0, tiled=True)  28.6 us
    all_to_all x2, starting transfers between devices, one_layer(): lax.all_to_all(jnp.einsum('secf,efd->secd', hidden, w_down, preferred_ele...  13.6 us
  transfers between devices with their start and end apart: 19, of which 13 were waited for; matrix products, arithmetic and copies ran while one was open for 4% of the time, Pallas kernels for 0%

commit v1 on v0

--- a/solution.py
+++ b/solution.py
@@ -84,7 +84,10 @@
         jnp.zeros((head_count, tok_rows, HEAD_DIM), jnp.float32),
     )
     empty_pages = jnp.zeros((blocks_dev, PAGE, 2, col_width), jnp.bfloat16)
-    piece = lax.all_gather(keys_vals, "tok", axis=0, tiled=True)
+    t1 = lax.axis_size("tok")
+    left_arr = jnp.stack([keys_vals] * t1)
+    everything = lax.all_to_all(left_arr, axis_name="tok", split_axis=0, concat_axis=0)
+    piece = jnp.concatenate(everything, 0)
     rows_key = piece.shape[0]
     step_rows = 1024
     while rows_key % step_rows != 0:

time: 636 us -> 733 us (1.15)
  local copies, waits for them, and re-layouts: 23.3 us -> 75.7 us
  starting transfers between devices: 47.2 us -> 76.6 us
    all_to_all x0 -> x2, waiting for transfers between devices: none -> 187 us  [one_layer(): lax.all_to_all(left_arr, axis_name='tok', split_axis=0, concat_axis=0)]
    all_gather x2 -> x0, waiting for transfers between devices: 164 us -> none  [one_layer(): piece = lax.all_gather(keys_vals, 'tok', axis=0, tiled=True)]
    while x8 -> x40, local copies, waits for them, and re-layouts: 0.02 us -> 23.8 us
    all_to_all x0 -> x2, starting transfers between devices: none -> 19.6 us  [one_layer(): lax.all_to_all(left_arr, axis_name='tok', split_axis=0, concat_axis=0)]
    slice x8, local copies, waits for them, and re-layouts: 10.2 us -> 26.3 us  [attend(): keys_vals[:, 1].reshape(rows_key, heads_here, head_size).astype(jnp.float32)]
    psum x2, starting transfers between devices: 0.08 us -> 11.6 us  [one_layer(): expert_total = lax.psum(expert_local, 'rep')]
    another operation x2 -> x4, local copies, waits for them, and re-layouts: 0.19 us -> 11.7 us  [the longest x2 11.5 us: one_layer(): left_arr = jnp.stack([keys_vals] * t1)]
    psum x2, waiting for transfers between devices: 98.6 us -> 91 us  [one_layer(): mid = resid + lax.psum(attn_part, 'rep')]
  transfers between devices with their start and end apart: 19 -> 19, of which waited for: 13 -> 13; matrix products, arithmetic and copies ran while one was open for 4% -> 6% of each run, Pallas kernels for 0% -> 0%
where the time goes in v1:
time: 733 us; the launch traced here: 727 us
  waiting for transfers between devices  455 us (62%)
  starting transfers between devices  76.6 us (10%)
  local copies, waits for them, and re-layouts  75.7 us (10%)
  blocking collectives  45.5 us (6%)
  matrix products  32.4 us (4%)
  other arithmetic  25.4 us (3%)
  between operations  15.4 us (2%)
    all_to_all x2, waiting for transfers between devices, one_layer(): lax.all_to_all(left_arr, axis_name='tok', split_axis=0, concat_axis=0)  187 us
    psum x2, waiting for transfers between devices, one_layer(): mid = resid + lax.psum(attn_part, 'rep')  91 us
    psum x2, waiting for transfers between devices, one_layer(): expert_total = lax.psum(expert_local, 'rep')  82.5 us
    all_to_all x2, waiting for transfers between devices, one_layer(): lax.all_to_all(jnp.einsum('secf,efd->secd', hidden, w_down, preferred_ele...  55.9 us
    all_to_all x1, blocking collectives, one_layer(): lax.all_to_all(copies, 'tok', split_axis=0, concat_axis=0, tiled=True)  45.5 us
    all_to_all x1, waiting for transfers between devices, one_layer(): lax.all_to_all(copies, 'tok', split_axis=0, concat_axis=0, tiled=True)  28.8 us
    slice x8, local copies, waits for them, and re-layouts, attend(): keys_vals[:, 1].reshape(rows_key, heads_here, head_size).astype(jnp.float32)  26.3 us
    while x40, local copies, waits for them, and re-layouts  23.8 us
  transfers between devices with their start and end apart: 19, of which 13 were waited for; matrix products, arithmetic and copies ran while one was open for 6% of the time, Pallas kernels for 0%

profile of v1, /device:TPU:1, one launch (start us, length us, event | category | flops | bytes accessed | tf_op | source)
XLA Modules:
  0.0 726.8 jit_solution(5404764835405888025)
XLA Ops:
  7.2 1.8 copy.61
  9.0 3.3 collective-permute-start.1
  12.5 2.9 collective-permute-done
  16.1 2.1 fusion.48
  18.5 5.7 stack.32
  24.2 9.8 %all-to-all-start = ((bf16[32,128,2,256]{3,2,1,0:T(2,128)(2,1)}), bf16[32,128,2,256]{3,2,1,0:T(2,128)(2,1)}, u32[]{:S(2)}, u32[]{:S(2)}) async-start(bf16[32,128,2,256]{3,2,1,0:T(2,128)(2,1)} %stack.32), calls=%async_computation | async-start | bytes 8388608 | tf_op jit(solution)/shard_map/all_to_all | solution.py:89
  36.5 96.9 %all-to-all-done = bf16[32,128,2,256]{3,2,1,0:T(2,128)(2,1)} async-done(((bf16[32,128,2,256]{3,2,1,0:T(2,128)(2,1)}), bf16[32,128,2,256]{3,2,1,0:T(2,128)(2,1)}, u32[]{:S(2)}, u32[]{:S(2)}) %all-to-all-start) | async-done | bytes 4194336 | tf_op jit(solution)/shard_map/all_to_all | solution.py:89
  133.3 35.8 %while.36 = (s32[]{:T(128)}, f32[4,128]{1,0:T(4,128)S(1)}, f32[4,128]{1,0:T(4,128)S(1)}, f32[4,128,64]{1,2,0:T(8,128)S(1)}, s32[128]{0:T(128)S(1)}, /*index=5*/s...) while((s32[]{:T(128)}, f32[4,128]{1,0:T(4,128)S(1)}, ...), condition=%wide.region_4.5_spmd.clone, body=%wide.region_1.4_spmd.clone.sunk | while | flops 476548736 | bytes 12441319 | solution.py:104
  133.7 3.3 constant_dynamic-slice_fusion.9
  138.3 1.3 copy.104
  140.8 1.4 fusion.180
  142.6 3.4 constant_dynamic-slice_fusion.9
  146.0 1.3 copy.103
  147.3 1.3 copy.104
  149.8 1.4 fusion.180
  151.7 3.3 constant_dynamic-slice_fusion.9
  154.9 1.3 copy.103
  158.8 1.4 fusion.180
  160.6 3.2 constant_dynamic-slice_fusion.9
  163.9 1.3 copy.103
  167.7 1.4 fusion.180
  169.2 2.3 fusion.86
  171.9 42.2 %all-reduce.5.cloned.1.call-done = f32[128,1024]{1,0:T(8,128)} async-done(((f32[128,1024]{1,0:T(8,128)}), f32[128,1024]{1,0:T(8,128)}) %all-reduce.5.cloned.1.call-update) | async-done | bytes 524304 | tf_op jit(solution)/shard_map/psum | solution.py:114
  217.0 1.4 broadcast_in_dim.165
  218.4 9.7 %all-to-all-start.1 = ((bf16[32,1,20,1024]{3,2,1,0:T(8,128)(2,1)}), bf16[32,1,20,1024]{3,2,1,0:T(8,128)(2,1)S(1)}, u32[]{:S(2)}, u32[]{:S(2)}) async-start(bf16[32,1,20,1024]{3,2,1,0:T(8,128)(2,1)} %bitcast.30), calls=%async_computation.1 | async-start | bytes 3145728 | tf_op jit(solution)/shard_map/all_to_all | solution.py:138
  228.1 3.2 collective-permute-start.5
  231.4 2.9 collective-permute-done.5
  234.3 28.8 %all-to-all-done.1 = bf16[32,1,20,1024]{3,2,1,0:T(8,128)(2,1)S(1)} async-done(((bf16[32,1,20,1024]{3,2,1,0:T(8,128)(2,1)}), bf16[32,1,20,1024]{3,2,1,0:T(8,128)(2,1)S(1)}, u32[]{:S(2)}, u32[]{:S(2)}) %all-to-all-start.1) | async-done | bytes 1310752 | tf_op jit(solution)/shard_map/all_to_all | solution.py:138
  263.1 3.2 convolution_bitcast_fusion.1
  266.4 2.1 fusion.42
  268.5 1.9 copy.67
  270.4 7.5 %all-to-all-start.2 = ((bf16[32,1,20,1024]{3,2,1,0:T(8,128)(2,1)}), bf16[32,1,20,1024]{3,2,1,0:T(8,128)(2,1)S(1)}, u32[]{:S(2)}, u32[]{:S(2)}) async-start(bf16[32,1,20,1024]{3,2,1,0:T(8,128)(2,1)} %copy.67), calls=%async_computation.2 | async-start | bytes 3145728 | tf_op jit(solution)/shard_map/all_to_all | solution.py:143
  277.9 11.4 %all-reduce.7.cloned.1.call-start = ((), (), s32[]{:S(2)}) async-start(), calls=%async_computation.7 | async-start | bytes 1048576 | tf_op jit(solution)/shard_map/psum | solution.py:158
  291.4 24.3 %all-to-all-done.2 = bf16[32,1,20,1024]{3,2,1,0:T(8,128)(2,1)S(1)} async-done(((bf16[32,1,20,1024]{3,2,1,0:T(8,128)(2,1)}), bf16[32,1,20,1024]{3,2,1,0:T(8,128)(2,1)S(1)}, u32[]{:S(2)}, u32[]{:S(2)}) %all-to-all-start.2) | async-done | bytes 1310752 | tf_op jit(solution)/shard_map/all_to_all | solution.py:143
  318.4 45.0 %all-reduce.7.cloned.1.call-done = f32[128,1024]{1,0:T(8,128)} async-done(((f32[128,1024]{1,0:T(8,128)}), f32[128,1024]{1,0:T(8,128)}) %all-reduce.7.cloned.1.call-update) | async-done | bytes 524304 | tf_op jit(solution)/shard_map/psum | solution.py:158
  365.7 5.8 stack.36
  371.5 9.8 %all-to-all-start.3 = ((bf16[32,128,2,256]{3,2,1,0:T(2,128)(2,1)}), bf16[32,128,2,256]{3,2,1,0:T(2,128)(2,1)}, u32[]{:S(2)}, u32[]{:S(2)}) async-start(bf16[32,128,2,256]{3,2,1,0:T(2,128)(2,1)} %stack.36), calls=%async_computation.3 | async-start | bytes 8388608 | tf_op jit(solution)/shard_map/all_to_all | solution.py:89
  381.4 89.7 %all-to-all-done.3 = bf16[32,128,2,256]{3,2,1,0:T(2,128)(2,1)} async-done(((bf16[32,128,2,256]{3,2,1,0:T(2,128)(2,1)}), bf16[32,128,2,256]{3,2,1,0:T(2,128)(2,1)}, u32[]{:S(2)}, u32[]{:S(2)}) %all-to-all-start.3) | async-done | bytes 4194336 | tf_op jit(solution)/shard_map/all_to_all | solution.py:89
  471.1 38.4 %while.37 = (s32[]{:T(128)}, f32[4,128]{1,0:T(4,128)S(1)}, f32[4,128]{1,0:T(4,128)S(1)}, f32[4,128,64]{1,2,0:T(8,128)}, s32[128]{0:T(128)S(1)}, /*index=5*/s32[4...) while((s32[]{:T(128)}, f32[4,128]{1,0:T(4,128)S(1)}, ...), condition=%wide.region_21.23_spmd.clone, body=%wide.region_18.22_spmd.clone.sunk | while | flops 476548736 | bytes 13489951 | solution.py:104
  471.5 3.2 constant_dynamic-slice_fusion.10
  474.7 1.3 copy.105
  478.6 1.4 fusion.187
  481.0 3.3 constant_dynamic-slice_fusion.10
  484.3 1.3 copy.105
  485.6 1.3 copy.106
  488.2 1.4 fusion.187
  490.6 3.4 constant_dynamic-slice_fusion.10
  494.0 1.3 copy.105
  497.9 1.4 fusion.187
  500.3 3.2 constant_dynamic-slice_fusion.10
  507.4 1.4 fusion.187
  510.4 2.1 fusion.84
  512.6 48.7 %all-reduce.9.cloned.1.call-done = f32[128,1024]{1,0:T(8,128)} async-done(((f32[128,1024]{1,0:T(8,128)}), f32[128,1024]{1,0:T(8,128)}) %all-reduce.9.cloned.1.call-update) | async-done | bytes 524304 | tf_op jit(solution)/shard_map/psum | solution.py:114
  564.3 45.5 %all_to_all.30 = bf16[32,1,20,1024]{3,2,1,0:T(8,128)(2,1)S(1)} all-to-all(bf16[32,1,20,1024]{3,2,1,0:T(8,128)(2,1)S(1)} %bitcast.260), channel_id=1, replica_groups=mesh['section'=2,'tok'=32,'rep'=4] {'tok'}, dimensions={0} | all-to-all | bytes 2621440 | tf_op jit(solution)/shard_map/all_to_all | solution.py:138
  609.9 1.8 convolution_bitcast_fusion
  612.7 2.0 copy.74
  614.7 6.2 all-to-all-start.5
  621.4 31.6 %all-to-all-done.5 = bf16[32,1,20,1024]{3,2,1,0:T(8,128)(2,1)S(1)} async-done(((bf16[32,1,20,1024]{3,2,1,0:T(8,128)(2,1)}), bf16[32,1,20,1024]{3,2,1,0:T(8,128)(2,1)S(1)}, u32[]{:S(2)}, u32[]{:S(2)}) %all-to-all-start.5) | async-done | bytes 1310752 | tf_op jit(solution)/shard_map/all_to_all | solution.py:143
  653.0 1.6 convert_reduce_fusion
  654.6 1.5 reshape.499
  660.6 9.9 %collective-permute-start.8 = (bf16[1,128,2,256]{3,2,1,0:T(2,128)(2,1)S(1)}, bf16[1,128,2,256]{3,2,1,0:T(2,128)(2,1)S(1)}, u32[]{:S(2)}, u32[]{:S(2)}) collective-permute-start(bf16[1,128,2,256]{3,2,1,0:T(2,128)(2,1)S(1)} %get-tuple-element.510), channel_id=1, source_target_pairs={{128,0},{129,1},{130,2},{131,3},{132,4},{133,5},{134,6},{135,7},{1... | collective-permute-start | bytes 393224 | tf_op jit(solution)/shard_map/ppermute | solution.py:203
  671.8 37.5 %all-reduce.11.cloned.1.call-done = f32[128,1024]{1,0:T(8,128)} async-done(((f32[128,1024]{1,0:T(8,128)}), f32[128,1024]{1,0:T(8,128)}) %all-reduce.11.cloned.1.call-update) | async-done | bytes 524304 | tf_op jit(solution)/shard_map/psum | solution.py:158
  714.1 3.7 collective-permute-done.9
  717.8 1.4 broadcast_select_fusion.2
  (241 shorter events, 54.2 us)
Async XLA Ops:
  7.2 29.2 %copy-start = (s32[2,4096]{1,0:T(2,128)S(1)}, s32[2,4096]{1,0:T(2,128)}, u32[]{:S(2)}) copy-start(s32[2,4096]{1,0:T(2,128)} %param.17) | copy-start | bytes 98308
  7.2 5.1 copy-start.19
  7.2 5.2 copy-start.4
  9.0 9.2 %copy-start.6 = (bf16[1,1024,3,256]{1,3,2,0:T(8,128)(2,1)}, bf16[1,1024,3,256]{1,3,2,0:T(8,128)(2,1)S(1)}, u32[]{:S(2)}) copy-start(bf16[1,1024,3,256]{1,3,2,0:T(8,128)(2,1)S(1)} %copy.61) | copy-start | bytes 4718596
  9.0 7.1 collective-permute-start.1
  12.3 3.2 collective-permute-start
  24.2 10.3 %copy-start.23 = (s32[2,128,2]{1,2,0:T(2,128)S(1)}, s32[2,128,2]{1,2,0:T(2,128)}, u32[]{:S(2)}) copy-start(s32[2,128,2]{1,2,0:T(2,128)} %param.18) | copy-start | bytes 6148
  24.2 109.1 %all-to-all-start = ((bf16[32,128,2,256]{3,2,1,0:T(2,128)(2,1)}), bf16[32,128,2,256]{3,2,1,0:T(2,128)(2,1)}, u32[]{:S(2)}, u32[]{:S(2)}) async-start(bf16[32,128,2,256]{3,2,1,0:T(2,128)(2,1)} %stack.32), calls=%async_computation | async-start | bytes 8388608 | tf_op jit(solution)/shard_map/all_to_all | solution.py:89
  34.0 180.1 %all-reduce.5.cloned.1.call-start = ((), (), s32[]{:S(2)}) async-start(), calls=%async_computation.6 | async-start | bytes 1048576 | tf_op jit(solution)/shard_map/psum | solution.py:114
  34.1 135.2 %collective-permute-start.2 = (bf16[256,1024]{1,0:T(8,128)(2,1)}, bf16[256,1024]{1,0:T(8,128)(2,1)}, u32[]{:S(2)}, u32[]{:S(2)}) collective-permute-start(bf16[256,1024]{1,0:T(8,128)(2,1)} %bitcast.12), channel_id=1, source_target_pairs={{0,128},{128,0},{1,129},{129,1},{2,130},{130,2},{3,131},{131,3},{4... | collective-permute-start | bytes 1572872 | tf_op jit(solution)/shard_map/ppermute | solution.py:187
  35.2 0.6 copy-start.17
  169.2 2.7 copy-start.11
  169.2 2.6 copy-start.16
  169.2 2.7 copy-start.18
  169.2 46.2 %copy-start.14 = (f32[1,1024]{1,0:T(1,128)S(1)}, f32[1,1024]{1,0:T(1,128)}, u32[]{:S(2)}) copy-start(f32[1,1024]{1,0:T(1,128)} %get-tuple-element.520) | copy-start | bytes 12292
  218.4 9.7 %copy-start.25 = (bf16[1,1,1024,2,352]{2,4,3,1,0:T(8,128)(2,1)S(1)}, bf16[1,1,1024,2,352]{2,4,3,1,0:T(8,128)(2,1)}, u32[]{:S(2)}) copy-start(bf16[1,1,1024,2,352]{2,4,3,1,0:T(8,128)(2,1)} %param.24) | copy-start | bytes 4325380
  218.4 44.8 %all-to-all-start.1 = ((bf16[32,1,20,1024]{3,2,1,0:T(8,128)(2,1)}), bf16[32,1,20,1024]{3,2,1,0:T(8,128)(2,1)S(1)}, u32[]{:S(2)}, u32[]{:S(2)}) async-start(bf16[32,1,20,1024]{3,2,1,0:T(8,128)(2,1)} %bitcast.30), calls=%async_computation.1 | async-start | bytes 3145728 | tf_op jit(solution)/shard_map/all_to_all | solution.py:138
  228.1 6.2 collective-permute-start.5
  231.3 35.0 %collective-permute-start.4 = (bf16[1,352,1024]{2,1,0:T(8,128)(2,1)}, bf16[1,352,1024]{2,1,0:T(8,128)(2,1)}, u32[]{:S(2)}, u32[]{:S(2)}) collective-permute-start(bf16[1,352,1024]{2,1,0:T(8,128)(2,1)} %bitcast.287), channel_id=1, source_target_pairs={{0,128},{128,0},{1,129},{129,1},{2,130},{130,2},{3,131},{131,3},{4... | collective-permute-start | bytes 2162696 | tf_op jit(solution)/shard_map/ppermute | solution.py:187
  263.1 3.2 copy-start.27
  270.4 18.9 %copy-start.10 = (bf16[1,1024,16]{1,2,0:T(8,128)(2,1)S(1)}, bf16[1,1024,16]{1,2,0:T(8,128)(2,1)}, u32[]{:S(2)}) copy-start(bf16[1,1024,16]{1,2,0:T(8,128)(2,1)} %param.23) | copy-start | bytes 98308
  270.4 20.9 %copy-start.15 = (s32[128,2]{0,1:T(2,128)S(1)}, s32[128,2]{0,1:T(2,128)}, u32[]{:S(2)}) copy-start(s32[128,2]{0,1:T(2,128)} %get-tuple-element.517) | copy-start | bytes 3076
  270.4 45.3 %all-to-all-start.2 = ((bf16[32,1,20,1024]{3,2,1,0:T(8,128)(2,1)}), bf16[32,1,20,1024]{3,2,1,0:T(8,128)(2,1)S(1)}, u32[]{:S(2)}, u32[]{:S(2)}) async-start(bf16[32,1,20,1024]{3,2,1,0:T(8,128)(2,1)} %copy.67), calls=%async_computation.2 | async-start | bytes 3145728 | tf_op jit(solution)/shard_map/all_to_all | solution.py:143
  277.9 85.6 %all-reduce.7.cloned.1.call-start = ((), (), s32[]{:S(2)}) async-start(), calls=%async_computation.7 | async-start | bytes 1048576 | tf_op jit(solution)/shard_map/psum | solution.py:158
  289.3 1.8 collective-permute-start.3
  290.3 27.0 %copy-start.20 = (pred[256]{0:T(512)(128)(4,1)}, pred[256]{0:T(512)(128)(4,1)S(1)}, u32[]{:S(2)}) copy-start(pred[256]{0:T(512)(128)(4,1)S(1)} %get-tuple-element.497) | copy-start | bytes 772
  317.3 46.2 %copy-start.3 = (f32[128,1024]{1,0:T(8,128)S(1)}, f32[128,1024]{1,0:T(8,128)}, u32[]{:S(2)}) copy-start(f32[128,1024]{1,0:T(8,128)} %all-reduce.5.cloned.1.call-done) | copy-start | bytes 1572868
  317.3 46.1 %copy-start.5 = (bf16[2,128,1024]{2,1,0:T(8,128)(2,1)S(1)}, bf16[2,128,1024]{2,1,0:T(8,128)(2,1)}, u32[]{:S(2)}) copy-start(bf16[2,128,1024]{2,1,0:T(8,128)(2,1)} %param.16) | copy-start | bytes 1572868
  317.5 47.2 %copy-start.7 = (bf16[1,1024,3,256]{1,3,2,0:T(8,128)(2,1)S(1)}, bf16[1,1024,3,256]{1,3,2,0:T(8,128)(2,1)}, u32[]{:S(2)}) copy-start(bf16[1,1024,3,256]{1,3,2,0:T(8,128)(2,1)} %copy-done.6) | copy-start | bytes 4718596
  317.5 47.2 %copy-start.22 = (f32[1,1024]{1,0:T(1,128)S(1)}, f32[1,1024]{1,0:T(1,128)}, u32[]{:S(2)}) copy-start(f32[1,1024]{1,0:T(1,128)} %get-tuple-element.513) | copy-start | bytes 12292
  371.5 99.6 %copy-start.12 = (s32[128]{0:T(128)S(1)}, s32[128]{0:T(128)}, u32[]{:S(2)}) copy-start(s32[128]{0:T(128)} %copy-done.11) | copy-start | bytes 1540
  371.5 99.6 %all-to-all-start.3 = ((bf16[32,128,2,256]{3,2,1,0:T(2,128)(2,1)}), bf16[32,128,2,256]{3,2,1,0:T(2,128)(2,1)}, u32[]{:S(2)}, u32[]{:S(2)}) async-start(bf16[32,128,2,256]{3,2,1,0:T(2,128)(2,1)} %stack.36), calls=%async_computation.3 | async-start | bytes 8388608 | tf_op jit(solution)/shard_map/all_to_all | solution.py:89
  381.3 180.0 %all-reduce.9.cloned.1.call-start = ((), (), s32[]{:S(2)}) async-start(), calls=%async_computation.8 | async-start | bytes 1048576 | tf_op jit(solution)/shard_map/psum | solution.py:114
  477.4 1.2 copy-start.8
  480.0 0.7 copy-start.9
  487.0 1.2 copy-start.8
  489.6 0.7 copy-start.9
  496.7 1.2 copy-start.8
  499.3 0.7 copy-start.9
  506.2 1.2 copy-start.8
  508.8 0.7 copy-start.9
  509.5 53.0 %copy-start.13 = (f32[1,1024]{1,0:T(1,128)S(1)}, f32[1,1024]{1,0:T(1,128)}, u32[]{:S(2)}) copy-start(f32[1,1024]{1,0:T(1,128)} %get-tuple-element.514) | copy-start | bytes 12292
  564.3 45.6 %copy-start.26 = (bf16[1,1,1024,2,352]{2,4,3,1,0:T(8,128)(2,1)S(1)}, bf16[1,1,1024,2,352]{2,4,3,1,0:T(8,128)(2,1)}, u32[]{:S(2)}) copy-start(bf16[1,1,1024,2,352]{2,4,3,1,0:T(8,128)(2,1)} %param.24) | copy-start | bytes 4325380
  609.9 1.8 copy-start.28
  614.7 38.3 %all-to-all-start.5 = ((bf16[32,1,20,1024]{3,2,1,0:T(8,128)(2,1)}), bf16[32,1,20,1024]{3,2,1,0:T(8,128)(2,1)S(1)}, u32[]{:S(2)}, u32[]{:S(2)}) async-start(bf16[32,1,20,1024]{3,2,1,0:T(8,128)(2,1)} %copy.74), calls=%async_computation.5 | async-start | bytes 3145728 | tf_op jit(solution)/shard_map/all_to_all | solution.py:143
  620.9 88.4 %all-reduce.11.cloned.1.call-start = ((), (), s32[]{:S(2)}) async-start(), calls=%async_computation.9 | async-start | bytes 1048576 | tf_op jit(solution)/shard_map/psum | solution.py:158
  656.1 1.1 copy-start.21
  657.2 1.1 copy-start.24
  657.2 52.2 %copy-start.2 = (f32[128,1024]{1,0:T(8,128)S(1)}, f32[128,1024]{1,0:T(8,128)}, u32[]{:S(2)}) copy-start(f32[128,1024]{1,0:T(8,128)} %all-reduce.9.cloned.1.call-done) | copy-start | bytes 1572868
  660.6 59.4 %copy-start.1 = (s32[2,4096]{1,0:T(2,128)S(1)}, s32[2,4096]{1,0:T(2,128)}, u32[]{:S(2)}) copy-start(s32[2,4096]{1,0:T(2,128)} %param.17) | copy-start | bytes 98308
  660.6 53.5 %collective-permute-start.8 = (bf16[1,128,2,256]{3,2,1,0:T(2,128)(2,1)S(1)}, bf16[1,128,2,256]{3,2,1,0:T(2,128)(2,1)S(1)}, u32[]{:S(2)}, u32[]{:S(2)}) collective-permute-start(bf16[1,128,2,256]{3,2,1,0:T(2,128)(2,1)S(1)} %get-tuple-element.510), channel_id=1, source_target_pairs={{128,0},{129,1},{130,2},{131,3},{132,4},{133,5},{134,6},{135,7},{1... | collective-permute-start | bytes 393224 | tf_op jit(solution)/shard_map/ppermute | solution.py:203
  670.5 48.7 %collective-permute-start.6 = (bf16[128,1024]{1,0:T(8,128)(2,1)S(1)}, bf16[128,1024]{1,0:T(8,128)(2,1)S(1)}, u32[]{:S(2)}, u32[]{:S(2)}) collective-permute-start(bf16[128,1024]{1,0:T(8,128)(2,1)S(1)} %get-tuple-element.496), channel_id=1, source_target_pairs={{128,0},{129,1},{130,2},{131,3},{132,4},{133,5},{134,6},{135,7},{1... | collective-permute-start | bytes 786440 | tf_op jit(solution)/shard_map/ppermute | solution.py:202
  710.5 8.7 %collective-permute-start.7 = (bf16[128,1024]{1,0:T(8,128)(2,1)S(1)}, bf16[128,1024]{1,0:T(8,128)(2,1)S(1)}, u32[]{:S(2)}, u32[]{:S(2)}) collective-permute-start(bf16[128,1024]{1,0:T(8,128)(2,1)S(1)} %add_convert_fusion), channel_id=1, source_target_pairs={{0,128},{1,129},{2,130},{3,131},{4,132},{5,133},{6,134},{7,135},{8... | collective-permute-start | bytes 786440 | tf_op jit(solution)/shard_map/ppermute | solution.py:204
  712.8 5.0 collective-permute-start.9
Sparse Core Ops, SparseCore 0:
  171.7 42.4 all-reduce.4
  318.6 44.8 all-reduce.6
  512.7 48.5 all-reduce.8
  658.4 50.8 all-reduce.10
